TPU v7x, 256 devices: a whole 4x4x8 slice. The times are simulated.
256 devices in a mesh: gx: 32 (over x, y, core), gy: 8 (over z).
Axes of the slice: x: 4, y: 4, z: 8, core: 2. Of those that a mesh axis runs over, the one named last changes fastest.
Arguments:
- orbitals: float32 [64, 128, 64, 128], P(None, 'gx', 'gy'), may hold values from -60 to 60, as said below
- potential: float32 [128, 64, 128], P('gx', 'gy'), may hold values from 0.2 to 2
Outputs:
- basis: float32 [64, 128, 64, 128], P(None, 'gx', 'gy')
- factor: float32 [64, 64], replicated
Inputs may be any that keep to these rules, and one draw needn't show every extreme that they name: `orbitals`: Real-valued entries.
All inputs are finite; a program needn't handle non-finite values.
Results may differ from a plain program's by a relative error of at most 0.00011.
Values sent between devices are 32-bit elements; how exact they have to be, the bound alone decides.
No kernel may reach another device: no remote copies, remote signals or barrier semaphores. Data moves between devices by JAX's collectives and lax.ppermute only.
A program may use at most 64 MiB of HBM per device.

v0:
```python
import jax
import jax.numpy as jnp
from jax import lax
from jax.sharding import PartitionSpec as P


def extended(cells, sides, width):
    for axis, dim in sides:
        count = lax.axis_size(axis)
        head = lax.slice_in_dim(cells, 0, width, axis=dim)
        tail = lax.slice_in_dim(cells, cells.shape[dim] - width, cells.shape[dim], axis=dim)
        cells = jnp.concatenate(
            [
                lax.ppermute(tail, axis, [(i, (i + 1) % count) for i in range(count)]),
                cells,
                lax.ppermute(head, axis, [((i + 1) % count, i) for i in range(count)]),
            ],
            axis=dim,
        )
    return cells


def apply_ham(padded, pot):
    core = padded[:, 2:-2, 2:-2]
    total = -7.5 * core
    total = total + 4.0 / 3.0 * (padded[:, 3:-1, 2:-2] + padded[:, 1:-3, 2:-2])
    total = total - 1.0 / 12.0 * (padded[:, 4:, 2:-2] + padded[:, :-4, 2:-2])
    total = total + 4.0 / 3.0 * (padded[:, 2:-2, 3:-1] + padded[:, 2:-2, 1:-3])
    total = total - 1.0 / 12.0 * (padded[:, 2:-2, 4:] + padded[:, 2:-2, :-4])
    total = total + 4.0 / 3.0 * (jnp.roll(core, 1, 3) + jnp.roll(core, -1, 3))
    total = total - 1.0 / 12.0 * (jnp.roll(core, 2, 3) + jnp.roll(core, -2, 3))
    return -0.5 * total + pot[None] * core


def with_faces(field):
    return extended(field, (("gx", 1), ("gy", 2)), 2)


def upper_factor(gram):
    order = gram.shape[0]
    index = jnp.arange(order)

    def column_step(col, lower):
        row_now = lax.dynamic_slice_in_dim(lower, col, 1, 0)[0]
        target = lax.dynamic_slice_in_dim(gram, col, 1, 1)[:, 0]
        column = target - jnp.dot(
            lower, row_now, precision=lax.Precision.HIGHEST, preferred_element_type=jnp.float32
        )
        pivot = jnp.sqrt(jnp.sum(jnp.where(index == col, column, 0.0)))
        values = jnp.where(index == col, pivot, column / pivot)
        values = jnp.where(index >= col, values, 0.0)
        return jnp.where(index[None, :] == col, values[:, None], lower)

    lower = lax.fori_loop(0, order, column_step, jnp.zeros_like(gram))
    return lower.T


def upper_inverse(upper):
    order = upper.shape[0]
    index = jnp.arange(order)

    def row_step(step, inverse):
        row = order - 1 - step
        upper_row = lax.dynamic_slice_in_dim(upper, row, 1, 0)[0]
        pivot = jnp.sum(jnp.where(index == row, upper_row, 0.0))
        rest = jnp.dot(
            upper_row, inverse, precision=lax.Precision.HIGHEST, preferred_element_type=jnp.float32
        )
        unit = jnp.where(index == row, 1.0, 0.0).astype(jnp.float32)
        new_row = (unit - rest) / pivot
        return jnp.where(index[:, None] == row, new_row[None, :], inverse)

    return lax.fori_loop(0, order, row_step, jnp.zeros_like(upper))


def shards(orbitals, potential):
    first = (apply_ham(with_faces(orbitals), potential) - 5.5 * orbitals) / 4.5
    applied = apply_ham(with_faces(first), potential)
    filtered = 2.0 * (applied - 5.5 * first) / 4.5 - orbitals
    width = filtered.shape[0]
    flat = filtered.reshape(width, -1)
    cells = flat.shape[1] * lax.axis_size("gx") * lax.axis_size("gy")
    local_gram = (
        jnp.dot(flat, flat.T, precision=lax.Precision.HIGHEST, preferred_element_type=jnp.float32)
        / cells
    )
    factor = upper_factor(lax.psum(local_gram, ("gx", "gy")))
    inverse = upper_inverse(factor)
    solved = jnp.dot(
        inverse.T, flat, precision=lax.Precision.HIGHEST, preferred_element_type=jnp.float32
    )
    basis = (solved * jnp.sqrt(jnp.float32(cells))).reshape(filtered.shape)
    return (basis, factor)


def solution(mesh):
    return jax.shard_map(
        shards,
        mesh=mesh,
        in_specs=(P(None, "gx", "gy", None), P("gx", "gy", None)),
        out_specs=(P(None, "gx", "gy", None), P()),
        check_vma=False,
    )
```

profile of v0, /device:TPU:1, one launch (start us, length us, event | category | flops | bytes accessed | tf_op | source)
XLA Modules:
  0.0 353.4 jit_solution(158170441676691293)
XLA Ops:
  0.6 2.4 fusion.60
  3.0 3.2 collective-permute-start
  8.3 4.5 %collective-permute-done = f32[64,2,8,128]{3,2,1,0:T(8,128)S(1)} collective-permute-done((f32[64,2,8,128]{3,2,1,0:T(8,128)}, f32[64,2,8,128]{3,2,1,0:T(8,128)S(1)}, u32[]{:S(2)}, u32[]{:S(2)}) %collective-permute-start) | collective-permute-done | bytes 524320 | tf_op jit(solution)/shard_map/ppermute | solution.py:16
  13.7 5.7 %collective-permute-start.2 = (f32[64,8,2,128]{3,1,2,0:T(8,128)S(1)}, f32[64,8,2,128]{3,1,2,0:T(8,128)S(1)}, u32[]{:S(2)}, u32[]{:S(2)}) collective-permute-start(f32[64,8,2,128]{3,1,2,0:T(8,128)S(1)} %get-tuple-element.266), channel_id=1, source_target_pairs={{1,0},{2,1},{3,2},{4,3},{5,4},{6,5},{7,6},{0,7},{9,8},{10,9},{11,1... | collective-permute-start | bytes 1572872 | tf_op jit(solution)/shard_map/ppermute | solution.py:16
  20.6 4.8 %collective-permute-done.2 = f32[64,8,2,128]{3,1,2,0:T(8,128)S(1)} collective-permute-done((f32[64,8,2,128]{3,1,2,0:T(8,128)S(1)}, f32[64,8,2,128]{3,1,2,0:T(8,128)S(1)}, u32[]{:S(2)}, u32[]{:S(2)}) %collective-permute-start.2) | collective-permute-done | bytes 524320 | tf_op jit(solution)/shard_map/ppermute | solution.py:16
  25.4 3.1 collective-permute-done.3
  28.6 7.3 %broadcast_multiply_fusion = (f32[64,4,8,128]{3,1,2,0:T(4,128)S(1)}, f32[64,4,8,128]{3,1,2,0:T(4,128)S(1)}) fusion(f32[64,4,8,128]{3,1,2,0:T(4,128)S(1)} %copy.55, f32[4,8,128]{2,0,1:T(4,128)S(1)} %copy.71, f32[64,4,8,2]{3,1,2,0:T(4,128)S(1)} %get-tuple-element.285, f32[64,4,8,126]{3,1,2,0:T(4,128)S(1)} %get-tuple-element.287, ...), kind=kLoop, calls=%fused_computation.105 | loop fusion | flops 11796480 | bytes 9453568 | tf_op jit(solution)/shard_map/div | solution.py:77
  36.4 9.8 %collective-permute-start.4 = (f32[64,2,8,128]{3,2,1,0:T(8,128)S(1)}, f32[64,2,8,128]{3,2,1,0:T(8,128)S(1)}, u32[]{:S(2)}, u32[]{:S(2)}) collective-permute-start(f32[64,2,8,128]{3,2,1,0:T(8,128)S(1)} %copy.74), channel_id=1, source_target_pairs={{8,0},{16,8},{24,16},{32,24},{40,32},{48,40},{56,48},{64,56},{72,6... | collective-permute-start | bytes 1572872 | tf_op jit(solution)/shard_map/ppermute | solution.py:16
  47.7 3.3 collective-permute-done.4
  51.3 1.3 collective-permute-done.5
  53.3 1.5 collective-permute-start.7
  56.0 5.3 %collective-permute-done.6 = f32[64,8,2,128]{3,1,2,0:T(8,128)S(1)} collective-permute-done((f32[64,8,2,128]{3,1,2,0:T(8,128)S(1)}, f32[64,8,2,128]{3,1,2,0:T(8,128)S(1)}, u32[]{:S(2)}, u32[]{:S(2)}) %collective-permute-start.6) | collective-permute-done | bytes 524320 | tf_op jit(solution)/shard_map/ppermute | solution.py:16
  61.3 1.3 collective-permute-done.7
  62.6 7.5 %multiply_subtract_fusion = f32[64,4,8,128]{3,1,2,0:T(4,128)S(1)} fusion(f32[64,4,8,128]{3,1,2,0:T(4,128)S(1)} %get-tuple-element.261, f32[64,4,8,2]{3,1,2,0:T(4,128)S(1)} %get-tuple-element.275, f32[64,4,8,126]{3,1,2,0:T(4,128)S(1)} %get-tuple-element.277, f32[64,4,8,126]{3,1,2,0:T(4,128)S(1)} %get-tuple-element.276, ...), kind=kLoop, calls=%fused_computation.97 | loop fusion | flops 12058624 | bytes 10502144 | tf_op jit(solution)/shard_map/sub | solution.py:79
  70.1 2.1 fusion.17
  72.2 81.9 %psum.7 = f32[64,64]{1,0:T(8,128)S(1)} all-reduce(f32[64,64]{1,0:T(8,128)S(1)} %fusion.17), channel_id=1, replica_groups=mesh['gx'=32,'gy'=8] {'gx','gy'}, use_global_device_ids=true, to_apply=%region_0.1 | all-reduce | flops 4096 | bytes 32768 | tf_op jit(solution)/shard_map/psum | solution.py:87
  154.2 101.3 %while.32 = (s32[]{:T(128)}, f32[64,64]{1,0:T(8,128)S(1)}, f32[64,64]{0,1:T(8,128)S(1)}, s32[]{:T(128)}, s32[]{:T(128)}) while((s32[]{:T(128)}, f32[64,64]{1,0:T(8,128)S(1)}, f32[64,64]{0,1:T(8,128)S(1)}, s32[]{:T(128)}, s32[]{:T(128)}) %tuple.94), condition=%wide.region_3.4_spmd.clone.clone, body=%wide.region_1.3_spmd.clone.clone.sunk | while | flops 62082 | bytes 102112 | solution.py:54
  255.6 95.1 %while.31 = (s32[]{:T(128)}, f32[64,64]{1,0:T(8,128)S(1)}, f32[64,64]{1,0:T(8,128)S(1)}, s32[]{:T(128)}, s32[]{:T(128)}, /*index=5*/s32[]{:T(128)}, s32[]{:T(128)}) while((s32[]{:T(128)}, f32[64,64]{1,0:T(8,128)S(1)}, f32[64,64]{1,0:T(8,128)S(1)}, s32[]{:T(128)}, s32[]{:T(128)}, /*index=5*/s32[]{:T(128)}, s32[]{:T(128)}) %tuple.100), condition=%wide.region_6.7_spmd.clone, body=%wide.region_4.6_spmd.clone.sunk | while | flops 61958 | bytes 67106 | solution.py:73
  256.2 0.8 fusion.75
  257.7 0.8 fusion.75
  259.1 0.8 fusion.75
  262.1 0.8 fusion.75
  263.6 0.8 fusion.75
  265.1 0.8 fusion.75
  266.6 0.8 fusion.75
  268.1 0.8 fusion.75
  271.0 0.8 fusion.75
  272.5 0.8 fusion.75
  274.0 0.8 fusion.75
  275.5 0.8 fusion.75
  277.0 0.8 fusion.75
  278.5 0.8 fusion.75
  279.9 0.8 fusion.75
  281.4 0.8 fusion.75
  282.9 0.8 fusion.75
  284.4 0.8 fusion.75
  285.9 0.8 fusion.75
  287.4 0.8 fusion.75
  290.3 0.8 fusion.75
  291.8 0.8 fusion.75
  293.3 0.8 fusion.75
  294.8 0.8 fusion.75
  296.3 0.8 fusion.75
  299.2 0.8 fusion.75
  300.7 0.8 fusion.75
  302.2 0.8 fusion.75
  350.6 1.6 fusion.16
  352.2 1.2 copy.89
  (585 shorter events, 137.0 us)
Async XLA Ops:
  0.6 5.6 %copy-start = (f32[64,4,8,128]{3,2,1,0:T(8,128)S(1)}, f32[64,4,8,128]{3,2,1,0:T(8,128)}, u32[]{:S(2)}) copy-start(f32[64,4,8,128]{3,2,1,0:T(8,128)} %param.6) | copy-start | bytes 3145732
  3.0 9.8 %collective-permute-start = (f32[64,2,8,128]{3,2,1,0:T(8,128)}, f32[64,2,8,128]{3,2,1,0:T(8,128)S(1)}, u32[]{:S(2)}, u32[]{:S(2)}) collective-permute-start(f32[64,2,8,128]{3,2,1,0:T(8,128)} %get-tuple-element.279), channel_id=1, source_target_pairs={{8,0},{16,8},{24,16},{32,24},{40,32},{48,40},{56,48},{64,56},{72,6... | collective-permute-start | bytes 1572872 | tf_op jit(solution)/shard_map/ppermute | solution.py:16
  6.2 0.7 copy-start.1
  6.2 6.8 %collective-permute-start.1 = (f32[64,2,8,128]{3,2,1,0:T(8,128)}, f32[64,2,8,128]{3,2,1,0:T(8,128)S(1)}, u32[]{:S(2)}, u32[]{:S(2)}) collective-permute-start(f32[64,2,8,128]{3,2,1,0:T(8,128)} %get-tuple-element.278), channel_id=1, source_target_pairs={{0,8},{8,16},{16,24},{24,32},{32,40},{40,48},{48,56},{56,64},{64,7... | collective-permute-start | bytes 1572872 | tf_op jit(solution)/shard_map/ppermute | solution.py:14
  13.7 11.8 %collective-permute-start.2 = (f32[64,8,2,128]{3,1,2,0:T(8,128)S(1)}, f32[64,8,2,128]{3,1,2,0:T(8,128)S(1)}, u32[]{:S(2)}, u32[]{:S(2)}) collective-permute-start(f32[64,8,2,128]{3,1,2,0:T(8,128)S(1)} %get-tuple-element.266), channel_id=1, source_target_pairs={{1,0},{2,1},{3,2},{4,3},{5,4},{6,5},{7,6},{0,7},{9,8},{10,9},{11,1... | collective-permute-start | bytes 1572872 | tf_op jit(solution)/shard_map/ppermute | solution.py:16
  19.3 9.2 %collective-permute-start.3 = (f32[64,8,2,128]{3,1,2,0:T(8,128)S(1)}, f32[64,8,2,128]{3,1,2,0:T(8,128)S(1)}, u32[]{:S(2)}, u32[]{:S(2)}) collective-permute-start(f32[64,8,2,128]{3,1,2,0:T(8,128)S(1)} %get-tuple-element.267), channel_id=1, source_target_pairs={{0,1},{1,2},{2,3},{3,4},{4,5},{5,6},{6,7},{7,0},{8,9},{9,10},{10,1... | collective-permute-start | bytes 1572872 | tf_op jit(solution)/shard_map/ppermute | solution.py:14
  36.4 14.6 %collective-permute-start.4 = (f32[64,2,8,128]{3,2,1,0:T(8,128)S(1)}, f32[64,2,8,128]{3,2,1,0:T(8,128)S(1)}, u32[]{:S(2)}, u32[]{:S(2)}) collective-permute-start(f32[64,2,8,128]{3,2,1,0:T(8,128)S(1)} %copy.74), channel_id=1, source_target_pairs={{8,0},{16,8},{24,16},{32,24},{40,32},{48,40},{56,48},{64,56},{72,6... | collective-permute-start | bytes 1572872 | tf_op jit(solution)/shard_map/ppermute | solution.py:16
  46.2 6.4 %collective-permute-start.5 = (f32[64,2,8,128]{3,2,1,0:T(8,128)S(1)}, f32[64,2,8,128]{3,2,1,0:T(8,128)S(1)}, u32[]{:S(2)}, u32[]{:S(2)}) collective-permute-start(f32[64,2,8,128]{3,2,1,0:T(8,128)S(1)} %copy.76), channel_id=1, source_target_pairs={{0,8},{8,16},{16,24},{24,32},{32,40},{40,48},{48,56},{56,64},{64,7... | collective-permute-start | bytes 1572872 | tf_op jit(solution)/shard_map/ppermute | solution.py:14
  53.2 8.1 %collective-permute-start.6 = (f32[64,8,2,128]{3,1,2,0:T(8,128)S(1)}, f32[64,8,2,128]{3,1,2,0:T(8,128)S(1)}, u32[]{:S(2)}, u32[]{:S(2)}) collective-permute-start(f32[64,8,2,128]{3,1,2,0:T(8,128)S(1)} %get-tuple-element.264), channel_id=1, source_target_pairs={{1,0},{2,1},{3,2},{4,3},{5,4},{6,5},{7,6},{0,7},{9,8},{10,9},{11,1... | collective-permute-start | bytes 1572872 | tf_op jit(solution)/shard_map/ppermute | solution.py:16
  53.3 9.3 %collective-permute-start.7 = (f32[64,8,2,128]{3,1,2,0:T(8,128)S(1)}, f32[64,8,2,128]{3,1,2,0:T(8,128)S(1)}, u32[]{:S(2)}, u32[]{:S(2)}) collective-permute-start(f32[64,8,2,128]{3,1,2,0:T(8,128)S(1)} %get-tuple-element.265), channel_id=1, source_target_pairs={{0,1},{1,2},{2,3},{3,4},{4,5},{5,6},{6,7},{7,0},{8,9},{9,10},{10,1... | collective-permute-start | bytes 1572872 | tf_op jit(solution)/shard_map/ppermute | solution.py:14
  350.6 1.6 copy-start.2
where the time goes:
time: 355 us; the launch traced here: 353 us
  matrix products  103 us (29%)
  blocking collectives  81.9 us (23%)
  other arithmetic  66.1 us (19%)
  loops' own time  46 us (13%)
  waiting for transfers between devices  23.6 us (7%)
  starting transfers between devices  20.4 us (6%)
  local copies, waits for them, and re-layouts  11.1 us (3%)
    psum x1, blocking collectives, shards(): factor = upper_factor(lax.psum(local_gram, ('gx', 'gy')))  81.9 us
    dot_general x64, matrix products, row_step(): jnp.dot(upper_row, inverse, precision=lax.Precision.HIGHEST, preferred_el...  50.1 us
    dot_general x64, matrix products, column_step(): jnp.dot(lower, row_now, precision=lax.Precision.HIGHEST, preferred_elemen...  49.5 us
    another operation x1, loops' own time, upper_factor(): lower = lax.fori_loop(0, order, column_step, jnp.zeros_like(gram))  45.6 us
    reduce_sum x64, other arithmetic, row_step(): pivot = jnp.sum(jnp.where(index == row, upper_row, 0.0))  39.3 us
    ppermute x4, starting transfers between devices, extended(): lax.ppermute(head, axis, [((i + 1) % count, i) for i in range(count)])  18.7 us
    ppermute x4, waiting for transfers between devices, extended(): lax.ppermute(head, axis, [((i + 1) % count, i) for i in range(count)])  17.9 us
    sub x1, other arithmetic, shards(): filtered = 2.0 * (applied - 5.5 * first) / 4.5 - orbitals  7.45 us
  transfers between devices with their start and end apart: 8, of which 7 were waited for; matrix products, arithmetic and copies ran while one was open for 2% of the time, Pallas kernels for 0%

commit v1 on v0

--- a/solution.py
+++ b/solution.py
@@ -84,7 +84,7 @@
         jnp.dot(flat, flat.T, precision=lax.Precision.HIGHEST, preferred_element_type=jnp.float32)
         / cells
     )
-    factor = upper_factor(lax.psum(local_gram, ("gx", "gy")))
+    factor = upper_factor(lax.psum(lax.psum(local_gram, "gx"), "gy"))
     inverse = upper_inverse(factor)
     solved = jnp.dot(
         inverse.T, flat, precision=lax.Precision.HIGHEST, preferred_element_type=jnp.float32

time: 355 us -> 432 us (1.22)
  the two profiles are of different devices: /device:TPU:1 before, /device:TPU:32 now
where the time goes in v1:
time: 432 us; the launch traced here: 430 us
  blocking collectives  152 us (35%)
  matrix products  103 us (24%)
  other arithmetic  66.1 us (15%)
  loops' own time  46 us (11%)
  waiting for transfers between devices  37.9 us (9%)
  starting transfers between devices  12.9 us (3%)
  local copies, waits for them, and re-layouts  11.1 us (3%)
    psum x2, blocking collectives, shards(): factor = upper_factor(lax.psum(lax.psum(local_gram, 'gx'), 'gy'))  152 us
    dot_general x64, matrix products, row_step(): jnp.dot(upper_row, inverse, precision=lax.Precision.HIGHEST, preferred_el...  50.1 us
    dot_general x64, matrix products, column_step(): jnp.dot(lower, row_now, precision=lax.Precision.HIGHEST, preferred_elemen...  49.5 us
    another operation x1, loops' own time, upper_factor(): lower = lax.fori_loop(0, order, column_step, jnp.zeros_like(gram))  45.6 us
    reduce_sum x64, other arithmetic, row_step(): pivot = jnp.sum(jnp.where(index == row, upper_row, 0.0))  39.3 us
    ppermute x4, waiting for transfers between devices, extended(): lax.ppermute(head, axis, [((i + 1) % count, i) for i in range(count)])  21.4 us
    ppermute x4, waiting for transfers between devices, extended(): lax.ppermute(tail, axis, [(i, (i + 1) % count) for i in range(count)])  16.5 us
    ppermute x4, starting transfers between devices, extended(): lax.ppermute(head, axis, [((i + 1) % count, i) for i in range(count)])  10.7 us
  transfers between devices with their start and end apart: 8, of which 8 were waited for; matrix products, arithmetic and copies ran while one was open for 1% of the time, Pallas kernels for 0%

profile of v1, /device:TPU:32, one launch (start us, length us, event | category | flops | bytes accessed | tf_op | source)
XLA Modules:
  0.0 430.5 jit_solution(14171137369367956073)
XLA Ops:
  0.6 2.3 fusion.60
  3.0 4.6 %collective-permute-start = (f32[64,2,8,128]{3,2,1,0:T(8,128)}, f32[64,2,8,128]{3,2,1,0:T(8,128)S(1)}, u32[]{:S(2)}, u32[]{:S(2)}) collective-permute-start(f32[64,2,8,128]{3,2,1,0:T(8,128)} %get-tuple-element.279), channel_id=1, source_target_pairs={{8,0},{16,8},{24,16},{32,24},{40,32},{48,40},{56,48},{64,56},{72,6... | collective-permute-start | bytes 1572872 | tf_op jit(solution)/shard_map/ppermute | solution.py:16
  9.7 5.0 %collective-permute-done = f32[64,2,8,128]{3,2,1,0:T(8,128)S(1)} collective-permute-done((f32[64,2,8,128]{3,2,1,0:T(8,128)}, f32[64,2,8,128]{3,2,1,0:T(8,128)S(1)}, u32[]{:S(2)}, u32[]{:S(2)}) %collective-permute-start) | collective-permute-done | bytes 524320 | tf_op jit(solution)/shard_map/ppermute | solution.py:16
  14.9 4.8 %collective-permute-done.1 = f32[64,2,8,128]{3,2,1,0:T(8,128)S(1)} collective-permute-done((f32[64,2,8,128]{3,2,1,0:T(8,128)}, f32[64,2,8,128]{3,2,1,0:T(8,128)S(1)}, u32[]{:S(2)}, u32[]{:S(2)}) %collective-permute-start.1) | collective-permute-done | bytes 524320 | tf_op jit(solution)/shard_map/ppermute | solution.py:14
  20.6 1.9 collective-permute-start.3
  23.8 5.9 %collective-permute-done.2 = f32[64,8,2,128]{3,1,2,0:T(8,128)S(1)} collective-permute-done((f32[64,8,2,128]{3,1,2,0:T(8,128)S(1)}, f32[64,8,2,128]{3,1,2,0:T(8,128)S(1)}, u32[]{:S(2)}, u32[]{:S(2)}) %collective-permute-start.2) | collective-permute-done | bytes 524320 | tf_op jit(solution)/shard_map/ppermute | solution.py:16
  29.6 3.9 collective-permute-done.3
  33.6 7.3 %broadcast_multiply_fusion = (f32[64,4,8,128]{3,1,2,0:T(4,128)S(1)}, f32[64,4,8,128]{3,1,2,0:T(4,128)S(1)}) fusion(f32[64,4,8,128]{3,1,2,0:T(4,128)S(1)} %copy.55, f32[4,8,128]{2,0,1:T(4,128)S(1)} %copy.71, f32[64,4,8,2]{3,1,2,0:T(4,128)S(1)} %get-tuple-element.285, f32[64,4,8,126]{3,1,2,0:T(4,128)S(1)} %get-tuple-element.287, ...), kind=kLoop, calls=%fused_computation.105 | loop fusion | flops 11796480 | bytes 9453568 | tf_op jit(solution)/shard_map/div | solution.py:77
  41.4 2.5 collective-permute-start.4
  45.5 5.1 %collective-permute-done.4 = f32[64,2,8,128]{3,2,1,0:T(8,128)S(1)} collective-permute-done((f32[64,2,8,128]{3,2,1,0:T(8,128)S(1)}, f32[64,2,8,128]{3,2,1,0:T(8,128)S(1)}, u32[]{:S(2)}, u32[]{:S(2)}) %collective-permute-start.4) | collective-permute-done | bytes 524320 | tf_op jit(solution)/shard_map/ppermute | solution.py:16
  50.9 5.2 %collective-permute-done.5 = f32[64,2,8,128]{3,2,1,0:T(8,128)S(1)} collective-permute-done((f32[64,2,8,128]{3,2,1,0:T(8,128)S(1)}, f32[64,2,8,128]{3,2,1,0:T(8,128)S(1)}, u32[]{:S(2)}, u32[]{:S(2)}) %collective-permute-start.5) | collective-permute-done | bytes 524320 | tf_op jit(solution)/shard_map/ppermute | solution.py:14
  56.8 3.3 collective-permute-start.6
  61.4 5.4 %collective-permute-done.6 = f32[64,8,2,128]{3,1,2,0:T(8,128)S(1)} collective-permute-done((f32[64,8,2,128]{3,1,2,0:T(8,128)S(1)}, f32[64,8,2,128]{3,1,2,0:T(8,128)S(1)}, u32[]{:S(2)}, u32[]{:S(2)}) %collective-permute-start.6) | collective-permute-done | bytes 524320 | tf_op jit(solution)/shard_map/ppermute | solution.py:16
  66.8 2.5 collective-permute-done.7
  69.3 7.5 %multiply_subtract_fusion = f32[64,4,8,128]{3,1,2,0:T(4,128)S(1)} fusion(f32[64,4,8,128]{3,1,2,0:T(4,128)S(1)} %get-tuple-element.261, f32[64,4,8,2]{3,1,2,0:T(4,128)S(1)} %get-tuple-element.275, f32[64,4,8,126]{3,1,2,0:T(4,128)S(1)} %get-tuple-element.277, f32[64,4,8,126]{3,1,2,0:T(4,128)S(1)} %get-tuple-element.276, ...), kind=kLoop, calls=%fused_computation.97 | loop fusion | flops 12058624 | bytes 10502144 | tf_op jit(solution)/shard_map/sub | solution.py:79
  76.8 2.1 fusion.17
  78.9 124.7 %psum.14 = f32[64,64]{1,0:T(8,128)S(1)} all-reduce(f32[64,64]{1,0:T(8,128)S(1)} %fusion.17), channel_id=1, replica_groups=mesh['gx'=32,'gy'=8] {'gx'}, use_global_device_ids=true, to_apply=%region_0.1 | all-reduce | flops 4096 | bytes 32768 | tf_op jit(solution)/shard_map/psum | solution.py:87
  203.6 27.5 %psum.15 = f32[64,64]{1,0:T(8,128)S(1)} all-reduce(f32[64,64]{1,0:T(8,128)S(1)} %psum.14), channel_id=1, replica_groups=mesh['gx'=32,'gy'=8] {'gy'}, use_global_device_ids=true, to_apply=%region_1.2 | all-reduce | flops 4096 | bytes 32768 | tf_op jit(solution)/shard_map/psum | solution.py:87
  231.2 101.3 %while.32 = (s32[]{:T(128)}, f32[64,64]{1,0:T(8,128)S(1)}, f32[64,64]{0,1:T(8,128)S(1)}, s32[]{:T(128)}, s32[]{:T(128)}) while((s32[]{:T(128)}, f32[64,64]{1,0:T(8,128)S(1)}, f32[64,64]{0,1:T(8,128)S(1)}, s32[]{:T(128)}, s32[]{:T(128)}) %tuple.94), condition=%wide.region_4.5_spmd.clone.clone, body=%wide.region_2.4_spmd.clone.clone.sunk | while | flops 62082 | bytes 102112 | solution.py:54
  332.6 95.1 %while.31 = (s32[]{:T(128)}, f32[64,64]{1,0:T(8,128)S(1)}, f32[64,64]{1,0:T(8,128)S(1)}, s32[]{:T(128)}, s32[]{:T(128)}, /*index=5*/s32[]{:T(128)}, s32[]{:T(128)}) while((s32[]{:T(128)}, f32[64,64]{1,0:T(8,128)S(1)}, f32[64,64]{1,0:T(8,128)S(1)}, s32[]{:T(128)}, s32[]{:T(128)}, /*index=5*/s32[]{:T(128)}, s32[]{:T(128)}) %tuple.100), condition=%wide.region_7.8_spmd.clone, body=%wide.region_5.7_spmd.clone.sunk | while | flops 61958 | bytes 67106 | solution.py:73
  333.2 0.8 fusion.75
  334.7 0.8 fusion.75
  336.2 0.8 fusion.75
  337.7 0.8 fusion.75
  339.2 0.8 fusion.75
  340.6 0.8 fusion.75
  342.1 0.8 fusion.75
  343.6 0.8 fusion.75
  345.1 0.8 fusion.75
  346.6 0.8 fusion.75
  349.6 0.8 fusion.75
  351.0 0.8 fusion.75
  352.5 0.8 fusion.75
  354.0 0.8 fusion.75
  355.5 0.8 fusion.75
  358.5 0.8 fusion.75
  359.9 0.8 fusion.75
  361.4 0.8 fusion.75
  362.9 0.8 fusion.75
  364.4 0.8 fusion.75
  365.9 0.8 fusion.75
  367.4 0.8 fusion.75
  368.9 0.8 fusion.75
  370.3 0.8 fusion.75
  371.8 0.8 fusion.75
  373.3 0.8 fusion.75
  427.7 1.6 fusion.16
  429.3 1.2 copy.89
  (586 shorter events, 138.7 us)
Async XLA Ops:
  0.6 7.0 %copy-start = (f32[64,4,8,128]{3,2,1,0:T(8,128)S(1)}, f32[64,4,8,128]{3,2,1,0:T(8,128)}, u32[]{:S(2)}) copy-start(f32[64,4,8,128]{3,2,1,0:T(8,128)} %param.6) | copy-start | bytes 3145732
  3.0 11.7 %collective-permute-start = (f32[64,2,8,128]{3,2,1,0:T(8,128)}, f32[64,2,8,128]{3,2,1,0:T(8,128)S(1)}, u32[]{:S(2)}, u32[]{:S(2)}) collective-permute-start(f32[64,2,8,128]{3,2,1,0:T(8,128)} %get-tuple-element.279), channel_id=1, source_target_pairs={{8,0},{16,8},{24,16},{32,24},{40,32},{48,40},{56,48},{64,56},{72,6... | collective-permute-start | bytes 1572872 | tf_op jit(solution)/shard_map/ppermute | solution.py:16
  7.6 0.7 copy-start.1
  7.6 12.1 %collective-permute-start.1 = (f32[64,2,8,128]{3,2,1,0:T(8,128)}, f32[64,2,8,128]{3,2,1,0:T(8,128)S(1)}, u32[]{:S(2)}, u32[]{:S(2)}) collective-permute-start(f32[64,2,8,128]{3,2,1,0:T(8,128)} %get-tuple-element.278), channel_id=1, source_target_pairs={{0,8},{8,16},{16,24},{24,32},{32,40},{40,48},{48,56},{56,64},{64,7... | collective-permute-start | bytes 1572872 | tf_op jit(solution)/shard_map/ppermute | solution.py:14
  20.4 9.3 %collective-permute-start.2 = (f32[64,8,2,128]{3,1,2,0:T(8,128)S(1)}, f32[64,8,2,128]{3,1,2,0:T(8,128)S(1)}, u32[]{:S(2)}, u32[]{:S(2)}) collective-permute-start(f32[64,8,2,128]{3,1,2,0:T(8,128)S(1)} %get-tuple-element.266), channel_id=1, source_target_pairs={{1,0},{2,1},{3,2},{4,3},{5,4},{6,5},{7,6},{0,7},{9,8},{10,9},{11,1... | collective-permute-start | bytes 1572872 | tf_op jit(solution)/shard_map/ppermute | solution.py:16
  20.6 13.0 %collective-permute-start.3 = (f32[64,8,2,128]{3,1,2,0:T(8,128)S(1)}, f32[64,8,2,128]{3,1,2,0:T(8,128)S(1)}, u32[]{:S(2)}, u32[]{:S(2)}) collective-permute-start(f32[64,8,2,128]{3,1,2,0:T(8,128)S(1)} %get-tuple-element.267), channel_id=1, source_target_pairs={{0,1},{1,2},{2,3},{3,4},{4,5},{5,6},{6,7},{7,0},{8,9},{9,10},{10,1... | collective-permute-start | bytes 1572872 | tf_op jit(solution)/shard_map/ppermute | solution.py:14
  41.4 9.2 %collective-permute-start.4 = (f32[64,2,8,128]{3,2,1,0:T(8,128)S(1)}, f32[64,2,8,128]{3,2,1,0:T(8,128)S(1)}, u32[]{:S(2)}, u32[]{:S(2)}) collective-permute-start(f32[64,2,8,128]{3,2,1,0:T(8,128)S(1)} %copy.74), channel_id=1, source_target_pairs={{8,0},{16,8},{24,16},{32,24},{40,32},{48,40},{56,48},{64,56},{72,6... | collective-permute-start | bytes 1572872 | tf_op jit(solution)/shard_map/ppermute | solution.py:16
  44.0 12.2 %collective-permute-start.5 = (f32[64,2,8,128]{3,2,1,0:T(8,128)S(1)}, f32[64,2,8,128]{3,2,1,0:T(8,128)S(1)}, u32[]{:S(2)}, u32[]{:S(2)}) collective-permute-start(f32[64,2,8,128]{3,2,1,0:T(8,128)S(1)} %copy.76), channel_id=1, source_target_pairs={{0,8},{8,16},{16,24},{24,32},{32,40},{40,48},{48,56},{56,64},{64,7... | collective-permute-start | bytes 1572872 | tf_op jit(solution)/shard_map/ppermute | solution.py:14
  56.8 10.0 %collective-permute-start.6 = (f32[64,8,2,128]{3,1,2,0:T(8,128)S(1)}, f32[64,8,2,128]{3,1,2,0:T(8,128)S(1)}, u32[]{:S(2)}, u32[]{:S(2)}) collective-permute-start(f32[64,8,2,128]{3,1,2,0:T(8,128)S(1)} %get-tuple-element.264), channel_id=1, source_target_pairs={{1,0},{2,1},{3,2},{4,3},{5,4},{6,5},{7,6},{0,7},{9,8},{10,9},{11,1... | collective-permute-start | bytes 1572872 | tf_op jit(solution)/shard_map/ppermute | solution.py:16
  60.1 9.2 %collective-permute-start.7 = (f32[64,8,2,128]{3,1,2,0:T(8,128)S(1)}, f32[64,8,2,128]{3,1,2,0:T(8,128)S(1)}, u32[]{:S(2)}, u32[]{:S(2)}) collective-permute-start(f32[64,8,2,128]{3,1,2,0:T(8,128)S(1)} %get-tuple-element.265), channel_id=1, source_target_pairs={{0,1},{1,2},{2,3},{3,4},{4,5},{5,6},{6,7},{7,0},{8,9},{9,10},{10,1... | collective-permute-start | bytes 1572872 | tf_op jit(solution)/shard_map/ppermute | solution.py:14
  427.7 1.6 copy-start.2
